TPU v7x, 512 devices: a whole 4x4x16 slice. The times are simulated.
512 devices in a mesh: rows: 32 (over x, y, core), cols: 16 (over z).
Axes of the slice: x: 4, y: 4, z: 16, core: 2. Of those that a mesh axis runs over, the one named last changes fastest.
Arguments:
- panel_t: float32 [256, 65536], P('cols', 'rows'), as said below
- trailing: float32 [65536, 4096], P('rows', 'cols'), may hold values from -6 to 6
- prev_lower_t: float32 [256, 65536], P('cols', 'rows'), may hold values from -6 to 6
- prev_upper: float32 [256, 4096], P(None, 'cols'), may hold values from -0.375 to 0.375
- leaf_picks: int32 [32, 256], P('rows'), may hold values from 0 to 2047, as said below
- merge_picks: int32 [31, 256], replicated, may hold values from 0 to 511, as said below
Outputs:
- lower_t: float32 [256, 65536], P('cols', 'rows')
- upper_left: float32 [256, 256], replicated
- upper_right: float32 [256, 4096], P(None, 'cols')
- updated: float32 [65536, 4096], P('rows', 'cols')
- gram: float32 [256, 256], P('cols')
Inputs may be any that keep to these rules, and one draw needn't show every extreme that they name: `leaf_picks`: each row lists 256 different row numbers within the 2048 rows of one index of rows. `merge_picks`: each row lists 256 different positions in a stack of two candidate lists. `panel_t`: the rows of the panel at the pivots form a strictly diagonally dominant block.
All inputs are finite; a program needn't handle non-finite values.
Results may differ from a plain program's by a relative error of at most 0.0003.
Values sent between devices are 32-bit elements; how exact they have to be, the bound alone decides.
No kernel may reach another device: no remote copies, remote signals or barrier semaphores. Data moves between devices by JAX's collectives and lax.ppermute only.
A program may use at most 64 MiB of HBM per device.

v0:
```python
import jax
import jax.numpy as jnp
from jax import lax
from jax.sharding import PartitionSpec as P

full_precision = lax.Precision.HIGHEST


def from_partner(shard, axis, apart):
    return lax.ppermute(shard, axis, [(i, i ^ 1 << apart) for i in range(lax.axis_size(axis))])


def trace_pivots(merge_picks, row_devices):
    list_width = merge_picks.shape[1]
    leaf_group = jnp.zeros((list_width,), jnp.int32)
    leaf_slot = jnp.arange(list_width, dtype=jnp.int32)
    levels = row_devices.bit_length() - 1
    for section in reversed(range(levels)):
        offset_rows = row_devices - (row_devices >> section)
        position = merge_picks[offset_rows + leaf_group, leaf_slot]
        right_side = (position >= list_width).astype(jnp.int32)
        leaf_group = 2 * leaf_group + right_side
        leaf_slot = position - list_width * right_side
    return (leaf_group, leaf_slot)


def product(left_side, right_side):
    return jnp.dot(left_side, right_side, precision=full_precision)


def unit_lower_inverse(lower):
    order = lower.shape[0]
    identity = jnp.eye(order, dtype=jnp.float32)
    power = identity - lower
    result = identity + power
    covered = 1
    while covered < order - 1:
        power = product(power, power)
        result = product(result, identity + power)
        covered = 2 * covered + 1
    return result


def upper_inverse(upper):
    diagonal = jnp.diagonal(upper)
    scaled = upper / diagonal[:, None]
    unit_inverse = unit_lower_inverse(scaled.T).T
    return unit_inverse / diagonal[None, :]


def small_factor(matrix):
    order = matrix.shape[0]
    row_index = lax.broadcasted_iota(jnp.int32, (order, order), 0)
    col_index = lax.broadcasted_iota(jnp.int32, (order, order), 1)
    line_index = jnp.arange(order, dtype=jnp.int32)
    reduced = matrix
    for column_index in range(order - 1):
        pivot_line = jnp.sum(jnp.where(row_index == column_index, reduced, 0.0), 0)
        pivot_column = jnp.sum(jnp.where(col_index == column_index, reduced, 0.0), 1)
        pivot_value = jnp.sum(jnp.where(line_index == column_index, pivot_line, 0.0))
        factors = jnp.where(line_index > column_index, pivot_column / pivot_value, 0.0)
        below = row_index > column_index
        reduced = jnp.where(
            below & (col_index > column_index),
            reduced - factors[:, None] * pivot_line[None, :],
            reduced,
        )
        reduced = jnp.where(below & (col_index == column_index), factors[:, None], reduced)
    return (jnp.tril(reduced, -1) + jnp.eye(order, dtype=matrix.dtype), jnp.triu(reduced))


def factor(matrix):
    order = matrix.shape[0]
    if order <= 32:
        return small_factor(matrix)
    middle_index = order // 2
    lower_head, upper_head = factor(matrix[:middle_index, :middle_index])
    upper_side = product(unit_lower_inverse(lower_head), matrix[:middle_index, middle_index:])
    lower_side = product(matrix[middle_index:, :middle_index], upper_inverse(upper_head))
    schur_block = matrix[middle_index:, middle_index:] - product(lower_side, upper_side)
    lower_tail, upper_tail = factor(schur_block)
    zero_upper = jnp.zeros((middle_index, order - middle_index), matrix.dtype)
    zero_lower = jnp.zeros((order - middle_index, middle_index), matrix.dtype)
    lower_full = jnp.concatenate(
        [
            jnp.concatenate([lower_head, zero_upper], 1),
            jnp.concatenate([lower_side, lower_tail], 1),
        ],
        0,
    )
    upper_full = jnp.concatenate(
        [
            jnp.concatenate([upper_head, upper_side], 1),
            jnp.concatenate([zero_lower, upper_tail], 1),
        ],
        0,
    )
    return (lower_full, upper_full)


def contract_first(left_side, right_side):
    return lax.dot_general(
        left_side, right_side, (((0,), (0,)), ((), ())), precision=full_precision
    )


def contract_second(left_side, right_side):
    return lax.dot_general(
        left_side, right_side, (((1,), (1,)), ((), ())), precision=full_precision
    )


def body(panel_t, trailing, prev_lower_t, prev_upper, leaf_picks, merge_picks):
    slab_rows = panel_t.shape[0]
    rows_here = panel_t.shape[1]
    row_devices = lax.axis_size("rows")
    own_row = lax.axis_index("rows")
    own_column = lax.axis_index("cols")
    leaf_group, leaf_slot = trace_pivots(merge_picks, row_devices)
    owner_mask = leaf_group == own_row
    local_rows = jnp.take(leaf_picks[0], leaf_slot)
    middle = trailing
    middle = middle - contract_first(
        lax.all_gather(prev_lower_t, "cols", axis=0, tiled=True), prev_upper
    )
    panel_full = lax.all_gather(panel_t, "cols", axis=0, tiled=True)
    middle, panel_full = (middle, panel_full)
    candidates = jnp.take(panel_t, leaf_picks[0], axis=1)
    levels = row_devices.bit_length() - 1
    for section in range(levels):
        partner = from_partner(candidates, "rows", section)
        upper_half = own_row >> section & 1
        stacked = jnp.where(
            upper_half == 0,
            jnp.concatenate([candidates, partner], 1),
            jnp.concatenate([partner, candidates], 1),
        )
        merge_index = row_devices - (row_devices >> section) + (own_row >> section + 1)
        selection = lax.dynamic_index_in_dim(merge_picks, merge_index, 0, keepdims=False)
        candidates = jnp.take(stacked, selection, axis=1)
    block_t = lax.all_gather(candidates, "cols", axis=0, tiled=True)
    lower_left, upper_left = factor(block_t.T)
    inverse = upper_inverse(upper_left)
    chosen_rows = jnp.take(middle, local_rows, axis=0)
    pivot_trailing = lax.psum(jnp.where(owner_mask[:, None], chosen_rows, 0.0), "rows")
    upper_right = product(unit_lower_inverse(lower_left), pivot_trailing)
    lower_full = jnp.dot(inverse.T, panel_full, precision=full_precision)
    lower_tile = lax.dynamic_slice_in_dim(lower_full, own_column * slab_rows, slab_rows, 0)
    updated = middle - contract_first(lower_full, upper_right)
    gram_rows = contract_second(lower_tile, lower_full)
    gram = lax.psum(gram_rows, "rows") / (rows_here * row_devices)
    return (lower_tile, upper_left, upper_right, updated, gram)


def solution(mesh):
    return jax.shard_map(
        body,
        mesh=mesh,
        in_specs=(
            P("cols", "rows"),
            P("rows", "cols"),
            P("cols", "rows"),
            P(None, "cols"),
            P("rows", None),
            P(),
        ),
        out_specs=(P("cols", "rows"), P(), P(None, "cols"), P("rows", "cols"), P("cols", None)),
        check_vma=False,
    )
```

profile of v0, /device:TPU:1, one launch (start us, length us, event | category | flops | bytes accessed | tf_op | source)
XLA Modules:
  0.0 666.7 jit_solution(18420080270595223450)
XLA Ops:
  9.2 2.5 gather_fusion.9
  11.8 2.3 gather_fusion.10
  14.1 2.3 gather_fusion.11
  16.5 2.3 gather_fusion.12
  18.9 2.3 gather_fusion.13
  22.2 8.8 %collective-permute-start = (f32[16,256]{0,1:T(8,128)S(1)}, f32[16,256]{0,1:T(8,128)S(1)}, u32[]{:S(2)}, u32[]{:S(2)}) collective-permute-start(f32[16,256]{0,1:T(8,128)S(1)} %select_bitcast_fusion.4), channel_id=1, source_target_pairs={{0,16},{16,0},{32,48},{48,32},{64,80},{80,64},{96,112},{112,96},{1... | collective-permute-start | bytes 49160 | tf_op jit(solution)/shard_map/ppermute | solution.py:10
  31.8 1.9 gather_fusion.14
  34.8 1.9 collective-permute-start.1
  36.7 5.1 collective-permute-done.1
  42.6 1.9 collective-permute-start.2
  44.6 5.7 collective-permute-done.2
  51.1 1.9 collective-permute-start.3
  53.1 3.8 collective-permute-done.3
  57.7 1.9 collective-permute-start.4
  60.2 4.8 collective-permute-done.4
  65.8 27.0 %all_gather.9 = f32[256,256]{1,0:T(8,128)S(1)} all-gather(f32[16,256]{1,0:T(8,128)S(1)} %select_bitcast_fusion.5), channel_id=1, replica_groups=mesh['rows'=32,'cols'=16] {'cols'}, dimensions={0}, use_global_device_ids=true | all-gather | bytes 278528 | tf_op jit(solution)/shard_map/all_gather | solution.py:141
  492.5 2.5 gather_fusion.8
  507.7 6.1 convolution_subtract_fusion.1
  515.7 3.5 fusion.224
  519.2 1.7 fusion.232
  520.9 127.3 %psum.15 = f32[16,256]{1,0:T(8,128)S(1)} all-reduce(f32[16,256]{1,0:T(8,128)S(1)} %fusion.232), channel_id=1, replica_groups=mesh['rows'=32,'cols'=16] {'rows'}, use_global_device_ids=true, to_apply=%region_745.747 | all-reduce | flops 4096 | bytes 32768 | tf_op jit(solution)/shard_map/psum | solution.py:151
  648.8 3.2 all-reduce.16.cloned.1.call-done
  652.0 1.3 fusion.231
  653.3 6.6 convolution_subtract_fusion
  (1113 shorter events, 419.9 us)
Async XLA Ops:
  7.2 500.5 %copy-start = (f32[256,256]{1,0:T(8,128)S(1)}, f32[256,256]{1,0:T(8,128)}, u32[]{:S(2)}) copy-start(f32[256,256]{1,0:T(8,128)} %param.11) | copy-start | bytes 786436
  7.2 4.6 copy-start.2
  7.2 500.5 %all-gather.5.cloned.1.call-start = ((), (), s32[]{:S(2)}) async-start(), calls=%async_computation.1 | async-start | bytes 2228224 | tf_op jit(solution)/shard_map/all_gather | solution.py:124
  7.9 507.7 %all-gather.3.cloned.1.call-start = ((), (), s32[]{:S(2)}) async-start(), calls=%async_computation | async-start | bytes 2228224 | tf_op jit(solution)/shard_map/all_gather | solution.py:126
  14.1 7.1 %copy-start.1 = (s32[1,256]{1,0:T(1,128)S(1)}, s32[1,256]{1,0:T(1,128)}, u32[]{:S(2)}) copy-start(s32[1,256]{1,0:T(1,128)} %param.12) | copy-start | bytes 3076
  22.2 11.7 %collective-permute-start = (f32[16,256]{0,1:T(8,128)S(1)}, f32[16,256]{0,1:T(8,128)S(1)}, u32[]{:S(2)}, u32[]{:S(2)}) collective-permute-start(f32[16,256]{0,1:T(8,128)S(1)} %select_bitcast_fusion.4), channel_id=1, source_target_pairs={{0,16},{16,0},{32,48},{48,32},{64,80},{80,64},{96,112},{112,96},{1... | collective-permute-start | bytes 49160 | tf_op jit(solution)/shard_map/ppermute | solution.py:10
  31.0 621.0 %all-reduce.16.cloned.1.call-start = ((), (), s32[]{:S(2)}) async-start(), calls=%async_computation.2 | async-start | bytes 524288 | tf_op jit(solution)/shard_map/psum | solution.py:145
  34.8 7.0 %collective-permute-start.1 = (f32[16,256]{0,1:T(8,128)S(1)}, f32[16,256]{0,1:T(8,128)S(1)}, u32[]{:S(2)}, u32[]{:S(2)}) collective-permute-start(f32[16,256]{0,1:T(8,128)S(1)} %select_bitcast_fusion.3), channel_id=1, source_target_pairs={{0,32},{16,48},{32,0},{48,16},{64,96},{80,112},{96,64},{112,80},{1... | collective-permute-start | bytes 49160 | tf_op jit(solution)/shard_map/ppermute | solution.py:10
  42.6 7.6 %collective-permute-start.2 = (f32[16,256]{0,1:T(8,128)S(1)}, f32[16,256]{0,1:T(8,128)S(1)}, u32[]{:S(2)}, u32[]{:S(2)}) collective-permute-start(f32[16,256]{0,1:T(8,128)S(1)} %select_bitcast_fusion.2), channel_id=1, source_target_pairs={{0,64},{16,80},{32,96},{48,112},{64,0},{80,16},{96,32},{112,48},{1... | collective-permute-start | bytes 49160 | tf_op jit(solution)/shard_map/ppermute | solution.py:10
  51.1 5.7 collective-permute-start.3
  57.7 7.3 %collective-permute-start.4 = (f32[16,256]{0,1:T(8,128)S(1)}, f32[16,256]{0,1:T(8,128)S(1)}, u32[]{:S(2)}, u32[]{:S(2)}) collective-permute-start(f32[16,256]{0,1:T(8,128)S(1)} %select_bitcast_fusion), channel_id=1, source_target_pairs={{0,256},{16,272},{32,288},{48,304},{64,320},{80,336},{96,352},{112... | collective-permute-start | bytes 49160 | tf_op jit(solution)/shard_map/ppermute | solution.py:10
  513.8 1.9 copy-start.3
  519.2 140.8 %copy-start.5 = (f32[16,2048]{1,0:T(8,128)}, f32[16,2048]{1,0:T(8,128)S(1)}, u32[]{:S(2)}) copy-start(f32[16,2048]{1,0:T(8,128)S(1)} %constant_dynamic-slice_fusion) | copy-start | bytes 393220
  653.3 6.6 copy-start.4
Sparse Core Ops, SparseCore 0:
  10.1 69.7 all-gather.4
  81.9 70.5 all-gather.2
  515.7 136.2 all-reduce.15
where the time goes:
time: 674 us; the launch traced here: 667 us
  other arithmetic  362 us (54%)
  blocking collectives  154 us (23%)
  matrix products  59.6 us (9%)
  local copies, waits for them, and re-layouts  33.2 us (5%)
  waiting for transfers between devices  23.2 us (3%)
  between operations  18.1 us (3%)
  starting transfers between devices  16.6 us (2%)
    select_n x248, other arithmetic, small_factor(): jnp.where(line_index > column_index, pivot_column / pivot_value, 0.0)  161 us
    reduce_sum x248, other arithmetic, small_factor(): jnp.sum(jnp.where(line_index == column_index, pivot_line, 0.0))  151 us
    psum x1, blocking collectives, body(): gram = lax.psum(gram_rows, 'rows') / (rows_here * row_devices)  127 us
    reduce_sum x244, other arithmetic, small_factor(): jnp.sum(jnp.where(col_index == column_index, reduced, 0.0), 1)  45.1 us
    dot_general x178, matrix products, product(): return jnp.dot(left_side, right_side, precision=full_precision)  41.6 us
    all_gather x1, blocking collectives, body(): block_t = lax.all_gather(candidates, 'cols', axis=0, tiled=True)  27 us
    ppermute x5, waiting for transfers between devices, from_partner(): lax.ppermute(shard, axis, [(i, i ^ 1 << apart) for i in range(lax.axis_si...  19.3 us
    ppermute x5, starting transfers between devices, from_partner(): lax.ppermute(shard, axis, [(i, i ^ 1 << apart) for i in range(lax.axis_si...  16.5 us
  transfers between devices with their start and end apart: 8, of which 5 were waited for; matrix products, arithmetic and copies ran while one was open for 67% of the time, Pallas kernels for 0%

commit v1 on v0

--- a/solution.py
+++ b/solution.py
@@ -148,7 +148,7 @@
     lower_tile = lax.dynamic_slice_in_dim(lower_full, own_column * slab_rows, slab_rows, 0)
     updated = middle - contract_first(lower_full, upper_right)
     gram_rows = contract_second(lower_tile, lower_full)
-    gram = lax.psum(gram_rows, "rows") / (rows_here * row_devices)
+    gram = jnp.sum(lax.all_gather(gram_rows, "rows"), axis=0) / (rows_here * row_devices)
     return (lower_tile, upper_left, upper_right, updated, gram)
 
 

time: 674 us -> 674 us (level)
  waiting for transfers between devices: 23.2 us -> 117 us
  blocking collectives: 154 us -> 61 us
    psum x1 -> x0, blocking collectives: 127 us -> none  [body(): gram = lax.psum(gram_rows, 'rows') / (rows_here * row_devices)]
    psum x1, waiting for transfers between devices: 3.17 us -> 96.5 us  [body(): lax.psum(jnp.where(owner_mask[:, None], chosen_rows, 0.0), 'rows')]
    all_gather x0 -> x1, blocking collectives: none -> 33.9 us  [body(): lax.all_gather(gram_rows, 'rows')]
where the time goes in v1:
time: 674 us; the launch traced here: 667 us
  other arithmetic  362 us (54%)
  waiting for transfers between devices  117 us (17%)
  blocking collectives  61 us (9%)
  matrix products  59.1 us (9%)
  local copies, waits for them, and re-layouts  33.3 us (5%)
  between operations  18.3 us (3%)
  starting transfers between devices  16.6 us (2%)
    select_n x248, other arithmetic, small_factor(): jnp.where(line_index > column_index, pivot_column / pivot_value, 0.0)  161 us
    reduce_sum x248, other arithmetic, small_factor(): jnp.sum(jnp.where(line_index == column_index, pivot_line, 0.0))  151 us
    psum x1, waiting for transfers between devices, body(): lax.psum(jnp.where(owner_mask[:, None], chosen_rows, 0.0), 'rows')  96.5 us
    reduce_sum x244, other arithmetic, small_factor(): jnp.sum(jnp.where(col_index == column_index, reduced, 0.0), 1)  45.1 us
    dot_general x178, matrix products, product(): return jnp.dot(left_side, right_side, precision=full_precision)  41.6 us
    all_gather x1, blocking collectives, body(): lax.all_gather(gram_rows, 'rows')  33.9 us
    all_gather x1, blocking collectives, body(): block_t = lax.all_gather(candidates, 'cols', axis=0, tiled=True)  27.1 us
    ppermute x5, waiting for transfers between devices, from_partner(): lax.ppermute(shard, axis, [(i, i ^ 1 << apart) for i in range(lax.axis_si...  19.3 us
  transfers between devices with their start and end apart: 8, of which 5 were waited for; matrix products, arithmetic and copies ran while one was open for 67% of the time, Pallas kernels for 0%

profile of v1, /device:TPU:1, one launch (start us, length us, event | category | flops | bytes accessed | tf_op | source)
XLA Modules:
  0.0 666.7 jit_solution(15844006773534883683)
XLA Ops:
  9.2 2.5 gather_fusion.9
  11.8 2.3 gather_fusion.10
  14.1 2.3 gather_fusion.11
  16.5 2.3 gather_fusion.12
  18.9 2.3 gather_fusion.13
  22.2 8.8 %collective-permute-start = (f32[16,256]{0,1:T(8,128)S(1)}, f32[16,256]{0,1:T(8,128)S(1)}, u32[]{:S(2)}, u32[]{:S(2)}) collective-permute-start(f32[16,256]{0,1:T(8,128)S(1)} %select_bitcast_fusion.4), channel_id=1, source_target_pairs={{0,16},{16,0},{32,48},{48,32},{64,80},{80,64},{96,112},{112,96},{1... | collective-permute-start | bytes 49160 | tf_op jit(solution)/shard_map/ppermute | solution.py:10
  31.8 1.9 gather_fusion.14
  34.8 1.9 collective-permute-start.1
  36.7 5.1 collective-permute-done.1
  42.6 1.9 collective-permute-start.2
  44.6 5.7 collective-permute-done.2
  51.1 1.9 collective-permute-start.3
  53.1 3.8 collective-permute-done.3
  57.7 1.9 collective-permute-start.4
  60.2 4.8 collective-permute-done.4
  65.8 27.1 %all_gather.15 = f32[256,256]{1,0:T(8,128)S(1)} all-gather(f32[16,256]{1,0:T(8,128)S(1)} %select_bitcast_fusion.5), channel_id=1, replica_groups=mesh['rows'=32,'cols'=16] {'cols'}, dimensions={0}, use_global_device_ids=true | all-gather | bytes 278528 | tf_op jit(solution)/shard_map/all_gather | solution.py:141
  492.6 2.6 gather_fusion.8
  507.8 5.9 convolution_subtract_fusion.1
  515.6 3.5 fusion.224
  519.2 1.7 fusion.232
  520.9 33.9 %all-gather = f32[512,256]{1,0:T(8,128)S(1)} all-gather(f32[16,256]{1,0:T(8,128)S(1)} %fusion.232), channel_id=2, replica_groups=mesh['rows'=32,'cols'=16] {'rows'}, dimensions={0}, use_global_device_ids=true | all-gather | bytes 540672 | tf_op jit(solution)/shard_map/all_gather | solution.py:151
  555.4 96.5 %all-reduce.16.cloned.1.call-done = f32[256,256]{1,0:T(8,128)} async-done(((f32[256,256]{1,0:T(8,128)}), f32[256,256]{1,0:T(8,128)}) %all-reduce.16.cloned.1.call-update) | async-done | bytes 262160 | tf_op jit(solution)/shard_map/psum | solution.py:145
  651.9 1.3 fusion.231
  653.3 6.5 convolution_subtract_fusion
  (1114 shorter events, 419.9 us)
Async XLA Ops:
  7.2 500.7 %copy-start = (f32[256,256]{1,0:T(8,128)S(1)}, f32[256,256]{1,0:T(8,128)}, u32[]{:S(2)}) copy-start(f32[256,256]{1,0:T(8,128)} %param.11) | copy-start | bytes 786436
  7.2 4.6 copy-start.2
  7.2 500.6 %all-gather.6.cloned.1.call-start = ((), (), s32[]{:S(2)}) async-start(), calls=%async_computation.1 | async-start | bytes 2228224 | tf_op jit(solution)/shard_map/all_gather | solution.py:124
  7.9 507.7 %all-gather.4.cloned.1.call-start = ((), (), s32[]{:S(2)}) async-start(), calls=%async_computation | async-start | bytes 2228224 | tf_op jit(solution)/shard_map/all_gather | solution.py:126
  14.1 7.1 %copy-start.1 = (s32[1,256]{1,0:T(1,128)S(1)}, s32[1,256]{1,0:T(1,128)}, u32[]{:S(2)}) copy-start(s32[1,256]{1,0:T(1,128)} %param.12) | copy-start | bytes 3076
  22.2 11.7 %collective-permute-start = (f32[16,256]{0,1:T(8,128)S(1)}, f32[16,256]{0,1:T(8,128)S(1)}, u32[]{:S(2)}, u32[]{:S(2)}) collective-permute-start(f32[16,256]{0,1:T(8,128)S(1)} %select_bitcast_fusion.4), channel_id=1, source_target_pairs={{0,16},{16,0},{32,48},{48,32},{64,80},{80,64},{96,112},{112,96},{1... | collective-permute-start | bytes 49160 | tf_op jit(solution)/shard_map/ppermute | solution.py:10
  31.0 620.9 %all-reduce.16.cloned.1.call-start = ((), (), s32[]{:S(2)}) async-start(), calls=%async_computation.2 | async-start | bytes 524288 | tf_op jit(solution)/shard_map/psum | solution.py:145
  34.8 7.0 %collective-permute-start.1 = (f32[16,256]{0,1:T(8,128)S(1)}, f32[16,256]{0,1:T(8,128)S(1)}, u32[]{:S(2)}, u32[]{:S(2)}) collective-permute-start(f32[16,256]{0,1:T(8,128)S(1)} %select_bitcast_fusion.3), channel_id=1, source_target_pairs={{0,32},{16,48},{32,0},{48,16},{64,96},{80,112},{96,64},{112,80},{1... | collective-permute-start | bytes 49160 | tf_op jit(solution)/shard_map/ppermute | solution.py:10
  42.6 7.6 %collective-permute-start.2 = (f32[16,256]{0,1:T(8,128)S(1)}, f32[16,256]{0,1:T(8,128)S(1)}, u32[]{:S(2)}, u32[]{:S(2)}) collective-permute-start(f32[16,256]{0,1:T(8,128)S(1)} %select_bitcast_fusion.2), channel_id=1, source_target_pairs={{0,64},{16,80},{32,96},{48,112},{64,0},{80,16},{96,32},{112,48},{1... | collective-permute-start | bytes 49160 | tf_op jit(solution)/shard_map/ppermute | solution.py:10
  51.1 5.7 collective-permute-start.3
  57.7 7.3 %collective-permute-start.4 = (f32[16,256]{0,1:T(8,128)S(1)}, f32[16,256]{0,1:T(8,128)S(1)}, u32[]{:S(2)}, u32[]{:S(2)}) collective-permute-start(f32[16,256]{0,1:T(8,128)S(1)} %select_bitcast_fusion), channel_id=1, source_target_pairs={{0,256},{16,272},{32,288},{48,304},{64,320},{80,336},{96,352},{112... | collective-permute-start | bytes 49160 | tf_op jit(solution)/shard_map/ppermute | solution.py:10
  513.8 1.9 copy-start.3
  519.1 140.6 %copy-start.5 = (f32[16,2048]{1,0:T(8,128)}, f32[16,2048]{1,0:T(8,128)S(1)}, u32[]{:S(2)}) copy-start(f32[16,2048]{1,0:T(8,128)S(1)} %constant_dynamic-slice_fusion) | copy-start | bytes 393220
  653.3 6.5 copy-start.4
Sparse Core Ops, SparseCore 0:
  10.1 69.6 all-gather.5
  81.9 70.4 all-gather.3
  515.7 136.1 all-reduce.15
